TPU v7x, 128 devices: a whole 4x4x4 slice. The times are simulated.
128 devices in a mesh: frow: 16 (over y, z), fcol: 8 (over x, core).
Axes of the slice: x: 4, y: 4, z: 4, core: 2. Of those that a mesh axis runs over, the one named last changes fastest.
Arguments:
- front_orig: float32 [16, 1024, 8, 2048], P('frow', None, 'fcol'), may hold values from -0.1 to 45, as said below
- child_tiles: bfloat16 [8192, 128, 128], P(('frow', 'fcol')), may hold values from -0.25 to 0.25
- tile_target: int32 [8192, 2], P(('frow', 'fcol')), may hold values from 0 to 127, as said below
- tile_rows: int32 [8192, 128], P(('frow', 'fcol')), may hold values from 0 to 127, each once within a row
- tile_cols: int32 [8192, 128], P(('frow', 'fcol')), may hold values from 0 to 127, each once within a row
Outputs:
- front_out: float32 [16, 1024, 8, 2048], P('frow', None, 'fcol')
Inputs may be any that keep to these rules, and one draw needn't show every extreme that they name: `front_orig`: Symmetric; the lower triangle of the front after every tile is added defines a positive definite matrix. `tile_target`: rows come 64 to a device in device order. Column 0 is the owner, frow index times 8 plus fcol index; column 1 the local block on that owner, local block row times 16 plus local block column; the block lies on or below the front's block diagonal. At most 2 tiles of one device go to one owner, and one owner receives exactly 2 from every device.
All inputs are finite; a program needn't handle non-finite values.
Results may differ from a plain program's by a relative error of at most 0.0003.
Values may be sent and summed in bfloat16 or wider, within the bound.
No kernel may reach another device: no remote copies, remote signals or barrier semaphores. Data moves between devices by JAX's collectives and lax.ppermute only.
A program may use at most 128 MiB of HBM per device.

v0:
```python
import jax
import jax.numpy as jnp
from jax import lax
from jax.sharding import PartitionSpec as P

PW = 512
NPANEL = 2
CAP = 2


def as_sent(x):
    return jax.tree.map(lambda a: a.astype(jnp.bfloat16) if a.dtype == jnp.float32 else a, x)


def broadcast(block, axis, source):
    block = jnp.where(lax.axis_index(axis) == source, block, jnp.zeros_like(block))
    return lax.psum(block, axis)


def place_tiles(received):
    tile_block, perm_block, target_block = received
    width = tile_block.shape[-1]
    positions = jnp.arange(width, dtype=jnp.int32)
    row_onehot = (perm_block[:, :, 0, None, :] == positions[:, None]).astype(jnp.bfloat16)
    col_onehot = (perm_block[:, :, 1, None, :] == positions[:, None]).astype(jnp.bfloat16)
    moved = jnp.einsum(
        "abxi,abij->abxj", row_onehot, tile_block, preferred_element_type=jnp.float32
    ).astype(jnp.bfloat16)
    placed = jnp.einsum(
        "abxj,abyj->abxy", moved, col_onehot, preferred_element_type=jnp.float32
    ).astype(jnp.bfloat16)
    return (placed, target_block)


def subtract_product(matrix, row_factor, col_factor):
    product = jnp.dot(
        row_factor, col_factor.T, precision=lax.Precision.HIGH, preferred_element_type=jnp.float32
    )
    return matrix - product


def shards(front_orig, child_tiles, tile_target, tile_rows, tile_cols):
    row_devs = lax.axis_size("frow")
    col_devs = lax.axis_size("fcol")
    owners = row_devs * col_devs
    row_here = lax.axis_index("frow")
    col_here = lax.axis_index("fcol")
    width = child_tiles.shape[1]
    held = child_tiles.shape[0]
    slot_count = owners * CAP
    owner_of = tile_target[:, 0]
    block_of = tile_target[:, 1]
    tile_order = jnp.arange(held, dtype=jnp.int32)
    same_owner = owner_of[:, None] == owner_of[None, :]
    earlier = tile_order[None, :] < tile_order[:, None]
    rank_of = jnp.sum(jnp.where(same_owner & earlier, 1, 0), axis=1).astype(jnp.int32)
    slot_of = owner_of * CAP + rank_of
    slot_match = slot_of[None, :] == jnp.arange(slot_count, dtype=jnp.int32)[:, None]
    source_tile = jnp.sum(jnp.where(slot_match, tile_order[None, :], 0), axis=1)
    filled = jnp.any(slot_match, axis=1)
    own_perms = jnp.stack([tile_rows, tile_cols], axis=1)
    placed_here, _ = place_tiles((child_tiles[None], own_perms[None], block_of[None]))
    placed_here = placed_here[0]
    send_tiles = jnp.where(
        filled[:, None, None],
        jnp.take(placed_here, source_tile, axis=0),
        jnp.zeros((), jnp.bfloat16),
    )
    send_blocks = jnp.where(filled, jnp.take(block_of, source_tile, axis=0), -1)
    placed = lax.all_to_all(
        send_tiles.reshape(owners, CAP, width, width),
        ("frow", "fcol"),
        split_axis=0,
        concat_axis=0,
        tiled=True,
    )
    blocks_in = lax.all_to_all(
        send_blocks.reshape(owners, CAP), ("frow", "fcol"), split_axis=0, concat_axis=0, tiled=True
    )
    local = front_orig[0, :, 0, :]
    row_blocks = local.shape[0] // width
    col_blocks = local.shape[1] // width
    block_ids = jnp.arange(row_blocks * col_blocks, dtype=jnp.int32)
    block_onehot = (blocks_in.reshape(1, slot_count) == block_ids[:, None]).astype(jnp.bfloat16)
    summed = jnp.dot(
        block_onehot, placed.reshape(slot_count, width * width), preferred_element_type=jnp.float32
    )
    added = (
        summed.reshape(row_blocks, col_blocks, width, width)
        .transpose(0, 2, 1, 3)
        .reshape(local.shape)
    )
    matrix = local + added
    first_ids = jnp.arange(row_blocks, dtype=jnp.int32) * col_blocks
    first_onehot = (blocks_in.reshape(1, slot_count) == first_ids[:, None]).astype(jnp.bfloat16)
    first_added = jnp.dot(
        first_onehot, placed.reshape(slot_count, width * width), preferred_element_type=jnp.float32
    ).reshape(local.shape[0], width)
    first_column = local[:, :width] + first_added
    local_rows = jnp.arange(local.shape[0], dtype=jnp.int32)
    local_cols = jnp.arange(local.shape[1], dtype=jnp.int32)
    global_rows = (local_rows // width * row_devs + row_here) * width + local_rows % width
    global_cols = (local_cols // width * col_devs + col_here) * width + local_cols % width
    total = NPANEL * PW
    hi = lax.Precision.HIGH
    first_row = lax.all_gather(
        first_column[:width].astype(jnp.bfloat16), "fcol", axis=1, tiled=True
    )[:, :total]
    split = total // 2
    left = lax.all_gather(first_row[:, :split], "frow", axis=0, tiled=True)[:total]
    left, right_src, matrix = lax.optimization_barrier((left, first_row[:, split:], matrix))
    right = lax.all_gather(right_src, "frow", axis=0, tiled=True)[:total]
    right, own_column = lax.optimization_barrier((right, first_column))
    halves = [left.astype(jnp.float32), right.astype(jnp.float32)]
    row_panel = lax.all_gather(own_column.astype(jnp.bfloat16), "fcol", axis=1, tiled=True)[
        :, :total
    ]
    half = row_devs // col_devs
    pairs = []
    for src_row in range(row_devs):
        for src_col in range(col_devs):
            dst_row = src_row // col_devs * col_devs + src_col
            dst_col = src_row % col_devs
            pairs.append((src_row * col_devs + src_col, dst_row * col_devs + dst_col))
    piece = lax.dynamic_slice_in_dim(row_panel, col_here * width, width, axis=0)
    piece = lax.ppermute(piece, ("frow", "fcol"), pairs)
    col_all = lax.all_gather(piece, "frow", axis=0, tiled=False)
    col_panel = (
        col_all.reshape(half, row_blocks, width, total)
        .transpose(1, 0, 2, 3)
        .reshape(local.shape[1], total)
    )
    rows_all = jnp.concatenate([row_panel, col_panel], axis=0).astype(jnp.float32)
    n_own = local.shape[0]
    full = lax.Precision.HIGHEST
    corner_blocks = total // width
    factor_full = jnp.zeros((total, total), jnp.float32)
    eye = jnp.eye(width, dtype=jnp.float32)
    inverses = []
    for h, cur in enumerate(halves):
        if h > 0:
            done_cols = factor_full[:, : h * split]
            cur = cur - jnp.dot(
                done_cols,
                done_cols[h * split : (h + 1) * split].T,
                precision=full,
                preferred_element_type=jnp.float32,
            )
        for b in range(split // width):
            start = h * split + b * width
            stop = start + width
            lb = b * width
            diag_block = cur[start:stop, lb : lb + width]
            symmetric = jnp.tril(diag_block) + jnp.tril(diag_block, -1).T
            factor = jnp.linalg.cholesky(symmetric)
            inverse = lax.linalg.triangular_solve(factor, eye, left_side=True, lower=True)
            inverses.append(inverse)
            factor_full = factor_full.at[start:stop, start:stop].set(factor)
            if stop < total:
                below = jnp.dot(
                    cur[stop:, lb : lb + width],
                    inverse.T,
                    precision=full,
                    preferred_element_type=jnp.float32,
                )
                factor_full = factor_full.at[stop:, start:stop].set(below)
                if lb + width < split:
                    cur = cur.at[stop:, lb + width :].add(
                        -jnp.dot(
                            below,
                            below[: split - lb - width].T,
                            precision=full,
                            preferred_element_type=jnp.float32,
                        )
                    )
    inv_blocks = jnp.stack(inverses)
    size = width
    while size < total:
        pairs_n = total // (2 * size)
        lower_left = jnp.stack(
            [
                factor_full[
                    (2 * k + 1) * size : (2 * k + 2) * size, 2 * k * size : (2 * k + 1) * size
                ]
                for k in range(pairs_n)
            ]
        )
        upper_inv = inv_blocks[0::2]
        lower_inv = inv_blocks[1::2]
        mixed = -jnp.einsum(
            "nab,nbc->nac",
            lower_inv,
            jnp.einsum("nab,nbc->nac", lower_left, upper_inv, precision=full),
            precision=full,
        )
        zeros = jnp.zeros_like(mixed)
        top = jnp.concatenate([upper_inv, zeros], axis=2)
        bottom = jnp.concatenate([mixed, lower_inv], axis=2)
        inv_blocks = jnp.concatenate([top, bottom], axis=1)
        size *= 2
    factor_inverse = inv_blocks[0]
    solved = jnp.dot(rows_all, factor_inverse.T, precision=hi, preferred_element_type=jnp.float32)
    row_factor = solved[:n_own]
    col_factor = solved[n_own:]
    matrix = subtract_product(matrix, row_factor, col_factor)
    corner_rows = lax.dynamic_slice_in_dim(
        factor_full, jnp.minimum(row_here, total // width - 1) * width, width, axis=0
    )
    head = jnp.where(row_here * width < total, corner_rows, row_factor[:width])
    panel_vals = jnp.concatenate([head, row_factor[width:]], axis=0)
    own_part = lax.dynamic_slice_in_dim(panel_vals, col_here * width, width, axis=1)
    matrix = matrix.at[:, :width].set(own_part)
    lower_part = global_rows[:, None] >= global_cols[None, :]
    result = jnp.where(lower_part, matrix, 0.0)
    return result[None, :, None, :]


def solution(mesh):
    return jax.shard_map(
        shards,
        mesh=mesh,
        in_specs=(
            P("frow", None, "fcol", None),
            P(("frow", "fcol"), None, None),
            P(("frow", "fcol"), None),
            P(("frow", "fcol"), None),
            P(("frow", "fcol"), None),
        ),
        out_specs=P("frow", None, "fcol", None),
        check_vma=False,
    )
```

profile of v0, /device:TPU:23, one launch (start us, length us, event | category | flops | bytes accessed | tf_op | source)
XLA Modules:
  0.0 611.7 jit_solution(1710537951863947196)
XLA Ops:
  11.4 10.6 %all-to-all-start = ((s32[128,1,2]{2,1,0:T(1,128)}), s32[128,1,2]{2,1,0:T(1,128)S(1)}, u32[]{:S(2)}, u32[]{:S(2)}) async-start(s32[128,1,2]{2,1,0:T(1,128)} %bitcast.5), calls=%async_computation | async-start | bytes 131072 | tf_op jit(solution)/shard_map/all_to_all | solution.py:77
  23.1 3.6 fusion.28
  26.8 10.2 %gather_fusion.1 = bf16[256,128,128]{2,1,0:T(8,128)(2,1)} fusion(bf16[64,128,128]{2,1,0:T(8,128)(2,1)} %fusion.28, s32[1024]{0:T(1024)S(1)} %pad_clamp_fusion), kind=kCustom, calls=%fused_computation.1 | custom fusion | bytes 16778240 | tf_op jit(solution)/shard_map/jit(_take)/gather | solution.py:66
  37.0 7.4 %select_select_fusion = bf16[128,2,128,128]{3,2,1,0:T(8,128)(2,1)} fusion(bf16[128,2,128,128]{3,2,1,0:T(8,128)(2,1)} %bitcast.217, pred[128,2]{1,0:T(8,128)(4,1)S(1)} %compare_and_fusion, pred[128,2]{1,0:T(8,128)(4,1)S(1)} %broadcast_in_dim.106), kind=kLoop, calls=%fused_computation.7 | loop fusion | flops 8388608 | bytes 16777728 | tf_op jit(solution)/shard_map/jit(_where)/select_n | solution.py:64
  44.4 10.2 %all-to-all-start.1 = ((bf16[128,2,128,128]{3,2,1,0:T(8,128)(2,1)}), bf16[128,2,128,128]{3,2,1,0:T(8,128)(2,1)}, u32[]{:S(2)}, u32[]{:S(2)}) async-start(bf16[128,2,128,128]{3,2,1,0:T(8,128)(2,1)} %select_select_fusion), calls=%async_computation.1 | async-start | bytes 16777216 | tf_op jit(solution)/shard_map/all_to_all | solution.py:70
  55.0 20.7 %copy.246 = f32[1,1024,1,2048]{1,3,2,0:T(8,128)} copy(f32[1,1024,1,2048]{3,2,1,0:T(1,128)} %param.52) | data formatting | bytes 16777216 | tf_op args[0]
  77.0 76.1 %all-to-all-done.1 = bf16[128,2,128,128]{3,2,1,0:T(8,128)(2,1)} async-done(((bf16[128,2,128,128]{3,2,1,0:T(8,128)(2,1)}), bf16[128,2,128,128]{3,2,1,0:T(8,128)(2,1)}, u32[]{:S(2)}, u32[]{:S(2)}) %all-to-all-start.1) | async-done | bytes 8388640 | tf_op jit(solution)/shard_map/all_to_all | solution.py:70
  153.1 7.8 %fusion.143 = f32[8,16384]{1,0:T(8,128)S(1)} fusion(s32[256]{0:T(256)S(1)} %eq.128, s32[8]{0:T(128)S(1)} %iota_multiply_fusion, bf16[32,8,128,128]{3,2,1,0:T(8,128)(2,1)} %bitcast.76), kind=kOutput, calls=%fused_computation.238 | convolution fusion | flops 67110912 | bytes 8913952 | tf_op jit(solution)/shard_map/dot_general | solution.py:96
  162.4 18.7 %all_gather.18 = bf16[128,1024]{0,1:T(8,128)(2,1)S(1)} all-gather(bf16[128,128]{0,1:T(8,128)(2,1)S(1)} %slice.839), channel_id=1, replica_groups=mesh['frow'=16,'fcol'=8] {'fcol'}, dimensions={1}, use_global_device_ids=true | all-gather | bytes 294912 | tf_op jit(solution)/shard_map/all_gather | solution.py:106
  184.6 23.3 %copy.365 = bf16[32,8,128,128]{3,1,2,0:T(8,128)(2,1)} copy(bf16[32,8,128,128]{3,2,1,0:T(8,128)(2,1)} %bitcast.76) | data formatting | bytes 16777216
  207.9 11.9 %copy.249 = bf16[256,16384]{0,1:T(8,128)(2,1)} copy(bf16[256,16384]{1,0:T(8,128)(2,1)} %bitcast.218) | data formatting | bytes 16777216 | tf_op jit(solution)/shard_map/reshape | solution.py:97
  219.8 6.3 %fusion.90 = f32[8,16,128,128]{3,1,2,0:T(8,128)S(1)} fusion(bf16[128,128,256,1]{2,1,0,3:T(8,128)(2,1)} %bitcast.221, s32[8,16]{1,0:T(8,128)S(1)} %multiply_add_fusion, s32[256]{0:T(256)S(1)} %eq.128), kind=kOutput, calls=%fused_computation.113 | convolution fusion | flops 1073774592 | bytes 16778752 | tf_op jit(solution)/shard_map/dot_general | solution.py:85
  226.1 7.5 %copy.364 = f32[128,8,16,128]{3,1,2,0:T(8,128)} copy(f32[128,8,16,128]{3,2,1,0:T(8,128)S(1)} %bitcast.222) | data formatting | bytes 16777216
  233.6 9.3 %copy.343 = f32[1024,2048]{0,1:T(8,128)} copy(f32[1024,2048]{1,0:T(8,128)} %bitcast.219) | data formatting | bytes 16777216 | tf_op jit(solution)/shard_map/reshape | solution.py:91
  242.9 12.1 %bitcast_add_fusion.16 = f32[1024,2048]{0,1:T(8,128)} fusion(f32[1024,2048]{0,1:T(8,128)} %copy.343, f32[1,1024,1,2048]{1,3,2,0:T(8,128)} %copy.246), kind=kLoop, calls=%fused_computation.280 | loop fusion | flops 2097152 | bytes 25165824 | tf_op jit(solution)/shard_map/add | solution.py:93
  257.4 11.7 %cholesky.134 = f32[128,128]{1,0:T(8,128)S(1)} custom-call(f32[128,128]{1,0:T(8,128)S(1)} %copy.258), custom_call_target="Cholesky" | custom-call | tf_op jit(solution)/shard_map/jit(cholesky)/cholesky | solution.py:155
  270.9 9.8 %custom-call.12 = f32[1,128,128]{1,2,0:T(8,128)S(1)} custom-call(f32[1,128,128]{2,1,0:T(8,128)S(1)} %copy.261), custom_call_target="InvertDiagBlocksLowerTriangular" | custom-call | tf_op jit(solution)/shard_map/triangular_solve/custom-call.0 | solution.py:156
  282.8 2.0 copy.289
  284.8 2.3 fusion.34
  288.2 11.9 %cholesky.145 = f32[128,128]{1,0:T(8,128)S(1)} custom-call(f32[128,128]{1,0:T(8,128)S(1)} %copy.268), custom_call_target="Cholesky" | custom-call | tf_op jit(solution)/shard_map/jit(cholesky)/cholesky | solution.py:155
  300.2 2.5 scatter.54
  305.8 9.8 %custom-call.13 = f32[1,128,128]{1,2,0:T(8,128)S(1)} custom-call(f32[1,128,128]{2,1,0:T(8,128)S(1)} %copy.271), custom_call_target="InvertDiagBlocksLowerTriangular" | custom-call | tf_op jit(solution)/shard_map/triangular_solve/custom-call.0 | solution.py:156
  318.6 11.7 %cholesky.156 = f32[128,128]{1,0:T(8,128)S(1)} custom-call(f32[128,128]{1,0:T(8,128)S(1)} %copy.278), custom_call_target="Cholesky" | custom-call | tf_op jit(solution)/shard_map/jit(cholesky)/cholesky | solution.py:155
  333.5 9.8 %custom-call.14 = f32[1,128,128]{1,2,0:T(8,128)S(1)} custom-call(f32[1,128,128]{2,1,0:T(8,128)S(1)} %copy.281), custom_call_target="InvertDiagBlocksLowerTriangular" | custom-call | tf_op jit(solution)/shard_map/triangular_solve/custom-call.0 | solution.py:156
  346.2 11.7 %cholesky.167 = f32[128,128]{1,0:T(8,128)S(1)} custom-call(f32[128,128]{1,0:T(8,128)S(1)} %fusion.105), custom_call_target="Cholesky" | custom-call | tf_op jit(solution)/shard_map/jit(cholesky)/cholesky | solution.py:155
  361.0 9.8 %custom-call.15 = f32[1,128,128]{1,2,0:T(8,128)S(1)} custom-call(f32[1,128,128]{2,1,0:T(8,128)S(1)} %copy.288), custom_call_target="InvertDiagBlocksLowerTriangular" | custom-call | tf_op jit(solution)/shard_map/triangular_solve/custom-call.0 | solution.py:156
  373.7 5.4 fusion.31
  381.7 11.7 %cholesky.178 = f32[128,128]{1,0:T(8,128)S(1)} custom-call(f32[128,128]{1,0:T(8,128)S(1)} %fusion.103), custom_call_target="Cholesky" | custom-call | tf_op jit(solution)/shard_map/jit(cholesky)/cholesky | solution.py:155
  395.6 9.8 %custom-call.16 = f32[1,128,128]{1,2,0:T(8,128)S(1)} custom-call(f32[1,128,128]{2,1,0:T(8,128)S(1)} %copy.299), custom_call_target="InvertDiagBlocksLowerTriangular" | custom-call | tf_op jit(solution)/shard_map/triangular_solve/custom-call.0 | solution.py:156
  408.1 2.1 collective-permute-start
  412.1 16.0 %collective-permute-done = bf16[128,1024]{0,1:T(8,128)(2,1)S(1)} collective-permute-done((bf16[128,1024]{0,1:T(8,128)(2,1)S(1)}, bf16[128,1024]{0,1:T(8,128)(2,1)S(1)}, u32[]{:S(2)}, u32[]{:S(2)}) %collective-permute-start) | collective-permute-done | bytes 262176 | tf_op jit(solution)/shard_map/ppermute | solution.py:126
  429.0 11.7 %cholesky.189 = f32[128,128]{1,0:T(8,128)S(1)} custom-call(f32[128,128]{1,0:T(8,128)S(1)} %fusion.101), custom_call_target="Cholesky" | custom-call | tf_op jit(solution)/shard_map/jit(cholesky)/cholesky | solution.py:155
  443.7 9.8 %custom-call.17 = f32[1,128,128]{1,2,0:T(8,128)S(1)} custom-call(f32[1,128,128]{2,1,0:T(8,128)S(1)} %copy.305), custom_call_target="InvertDiagBlocksLowerTriangular" | custom-call | tf_op jit(solution)/shard_map/triangular_solve/custom-call.0 | solution.py:156
  454.9 11.7 %cholesky.200 = f32[128,128]{1,0:T(8,128)S(1)} custom-call(f32[128,128]{1,0:T(8,128)S(1)} %fusion.99), custom_call_target="Cholesky" | custom-call | tf_op jit(solution)/shard_map/jit(cholesky)/cholesky | solution.py:155
  469.5 10.0 %custom-call.18 = f32[1,128,128]{1,2,0:T(8,128)S(1)} custom-call(f32[1,128,128]{2,1,0:T(8,128)S(1)} %copy.311), custom_call_target="InvertDiagBlocksLowerTriangular" | custom-call | tf_op jit(solution)/shard_map/triangular_solve/custom-call.0 | solution.py:156
  480.8 11.7 %cholesky.211 = f32[128,128]{1,0:T(8,128)S(1)} custom-call(f32[128,128]{1,0:T(8,128)S(1)} %fusion.97), custom_call_target="Cholesky" | custom-call | tf_op jit(solution)/shard_map/jit(cholesky)/cholesky | solution.py:155
  493.8 9.8 %custom-call.19 = f32[1,128,128]{1,2,0:T(8,128)S(1)} custom-call(f32[1,128,128]{2,1,0:T(8,128)S(1)} %get-tuple-element.281), custom_call_target="InvertDiagBlocksLowerTriangular" | custom-call | tf_op jit(solution)/shard_map/triangular_solve/custom-call.0 | solution.py:156
  510.9 3.5 fusion.42
  517.8 2.9 copy.252
  520.7 5.6 copy.360
  526.2 6.7 %copy.251 = bf16[2,8,128,1024]{3,2,0,1:T(8,128)(2,1)} copy(bf16[2,8,128,1024]{2,1,0,3:T(8,128)(2,1)} %bitcast.220) | data formatting | bytes 8388608 | tf_op jit(solution)/shard_map/reshape | solution.py:129
  532.9 16.6 %fusion.2 = f32[3072,1024]{1,0:T(8,128)S(1)} fusion(bf16[2048,1024]{1,0:T(8,128)(2,1)} %bitcast.224, bf16[1024,1024]{1,0:T(8,128)(2,1)S(1)} %copy.252, f32[1,512,512]{2,1,0:T(8,128)} %get-tuple-element.292, f32[1,512,512]{2,1,0:T(8,128)} %get-tuple-element.291, f32[1,512,512]{2,1,0:T(8,128)S(1)} %fusion.35), kind=kOutput, calls=%fused_computation.8 | convolution fusion | flops 19344130048 | bytes 22020096 | tf_op jit(solution)/shard_map/dot_general | solution.py:202
  549.6 2.3 slice.757
  551.9 17.7 %fusion.15 = f32[1024,2048]{0,1:T(8,128)} fusion(f32[1024,2048]{0,1:T(8,128)} %bitcast_add_fusion.16, f32[3072,1024]{1,0:T(8,128)S(1)} %fusion.2), kind=kOutput, calls=%fused_computation.26 | convolution fusion | flops 12886999040 | bytes 29360128 | tf_op jit(solution)/shard_map/dot_general | solution.py:36
  569.8 5.0 copy.345
  575.9 2.6 fusion.49
  578.5 5.9 select_bitcast_fusion
  584.5 20.5 %copy.329 = f32[1,1024,1,2048]{3,2,1,0:T(1,128)} copy(f32[1,1024,1,2048]{1,3,2,0:T(8,128)} %select_bitcast_fusion) | data formatting | bytes 16777216 | tf_op jit(solution)/shard_map/broadcast_in_dim | solution.py:215
  (208 shorter events, 69.3 us)
Async XLA Ops:
  6.5 16.6 %copy-start = (bf16[64,128,128]{2,1,0:T(8,128)(2,1)S(1)}, bf16[64,128,128]{2,1,0:T(8,128)(2,1)}, u32[]{:S(2)}) copy-start(bf16[64,128,128]{2,1,0:T(8,128)(2,1)} %param.53) | copy-start | bytes 6291460
  11.4 33.0 %all-to-all-start = ((s32[128,1,2]{2,1,0:T(1,128)}), s32[128,1,2]{2,1,0:T(1,128)S(1)}, u32[]{:S(2)}, u32[]{:S(2)}) async-start(s32[128,1,2]{2,1,0:T(1,128)} %bitcast.5), calls=%async_computation | async-start | bytes 131072 | tf_op jit(solution)/shard_map/all_to_all | solution.py:77
  44.4 108.7 %all-to-all-start.1 = ((bf16[128,2,128,128]{3,2,1,0:T(8,128)(2,1)}), bf16[128,2,128,128]{3,2,1,0:T(8,128)(2,1)}, u32[]{:S(2)}, u32[]{:S(2)}) async-start(bf16[128,2,128,128]{3,2,1,0:T(8,128)(2,1)} %select_select_fusion), calls=%async_computation.1 | async-start | bytes 16777216 | tf_op jit(solution)/shard_map/all_to_all | solution.py:70
  54.6 200.4 %all-gather.6.cloned.1.call-start = ((), (), s32[]{:S(2)}) async-start(), calls=%async_computation.2 | async-start | bytes 2228224 | tf_op jit(solution)/shard_map/all_gather | solution.py:110
  162.3 45.6 %copy-start.5 = (bf16[1024,128]{0,1:T(8,128)(2,1)}, bf16[1024,128]{0,1:T(8,128)(2,1)S(1)}, u32[]{:S(2)}) copy-start(bf16[1024,128]{0,1:T(8,128)(2,1)S(1)} %slice_add_fusion) | copy-start | bytes 786436
  181.8 162.5 %all-gather.8.cloned.1.call-start = ((), (), s32[]{:S(2)}) async-start(), calls=%async_computation.3 | async-start | bytes 2228224 | tf_op jit(solution)/shard_map/all_gather | solution.py:112
  181.9 26.0 %copy-start.10 = (s32[128]{0:T(128)}, s32[128]{0:T(128)S(1)}, u32[]{:S(2)}) copy-start(s32[128]{0:T(128)S(1)} %iota_add_fusion) | copy-start | bytes 1540
  182.1 75.1 %copy-start.6 = (pred[128,128]{0,1:T(8,128)(4,1)}, pred[128,128]{0,1:T(8,128)(4,1)S(1)}, u32[]{:S(2)}) copy-start(pred[128,128]{0,1:T(8,128)(4,1)S(1)} %copy.255) | copy-start | bytes 49156
  256.6 150.5 %all-gather.10.cloned.1.call-start = ((), (), s32[]{:S(2)}) async-start(), calls=%async_computation.4 | async-start | bytes 2359296 | tf_op jit(solution)/shard_map/all_gather | solution.py:115
  287.1 16.4 %copy-start.4 = (f32[896,128]{0,1:T(8,128)S(1)}, f32[896,128]{0,1:T(8,128)}, u32[]{:S(2)}) copy-start(f32[896,128]{0,1:T(8,128)} %copy.289) | copy-start | bytes 1376260
  300.2 18.2 %copy-start.7 = (pred[128,128]{0,1:T(8,128)(4,1)S(1)}, pred[128,128]{0,1:T(8,128)(4,1)}, u32[]{:S(2)}) copy-start(pred[128,128]{0,1:T(8,128)(4,1)} %copy-done.6) | copy-start | bytes 49156
  318.3 27.7 %copy-start.11 = (s32[128]{0:T(128)S(1)}, s32[128]{0:T(128)}, u32[]{:S(2)}) copy-start(s32[128]{0:T(128)} %copy-done.10) | copy-start | bytes 1540
  344.3 28.5 %slice-start = ((bf16[2048,512]{0,1:T(8,128)(2,1)}), bf16[1024,512]{0,1:T(8,128)(2,1)S(1)}, s32[]{:S(2)}) async-start(bf16[2048,512]{0,1:T(8,128)(2,1)} %all-gather.8.cloned.1.call-done), calls=%async_computation.6 | async-start | bytes 2097152 | tf_op jit(solution)/shard_map/slice | solution.py:112
  344.3 176.3 %all-gather.12.cloned.1.call-start = ((), (), s32[]{:S(2)}) async-start(), calls=%async_computation.5 | async-start | bytes 4456448 | tf_op jit(solution)/shard_map/all_gather | solution.py:127
  373.7 31.7 %copy-start.3 = (f32[8,128,128]{2,1,0:T(8,128)S(1)}, f32[8,128,128]{2,1,0:T(8,128)}, u32[]{:S(2)}) copy-start(f32[8,128,128]{2,1,0:T(8,128)} %get-tuple-element.321) | copy-start | bytes 1572868
  379.2 1.4 copy-start.2
  408.1 19.9 %collective-permute-start = (bf16[128,1024]{0,1:T(8,128)(2,1)S(1)}, bf16[128,1024]{0,1:T(8,128)(2,1)S(1)}, u32[]{:S(2)}, u32[]{:S(2)}) collective-permute-start(bf16[128,1024]{0,1:T(8,128)(2,1)S(1)} %constant_dynamic-slice_fusion), channel_id=1, source_target_pairs={{0,0},{1,8},{2,16},{3,24},{4,32},{5,40},{6,48},{7,56},{8,1},{9,9},... | collective-permute-start | bytes 786440 | tf_op jit(solution)/shard_map/ppermute | solution.py:126
  428.0 0.7 copy-start.8
  574.8 3.7 copy-start.9
  574.8 3.7 copy-start.12
  578.5 26.4 %copy-start.1 = (bf16[64,128,128]{2,1,0:T(8,128)(2,1)S(1)}, bf16[64,128,128]{2,1,0:T(8,128)(2,1)}, u32[]{:S(2)}) copy-start(bf16[64,128,128]{2,1,0:T(8,128)(2,1)} %param.53) | copy-start | bytes 6291460
Sparse Core Ops, SparseCore 0:
  181.9 45.7 all-gather.5
  256.8 45.8 all-gather.7
  344.4 24.9 all-gather.9
  428.9 53.5 all-gather.11
where the time goes:
time: 620 us; the launch traced here: 612 us
  other arithmetic  227 us (37%)
  local copies, waits for them, and re-layouts  154 us (25%)
  waiting for transfers between devices  92.2 us (15%)
  matrix products  82.1 us (13%)
  starting transfers between devices  24 us (4%)
  blocking collectives  18.7 us (3%)
  between operations  14.5 us (2%)
    another operation x24, other arithmetic, shards(): factor = jnp.linalg.cholesky(symmetric)  100 us
    another operation x11, other arithmetic, shards(): lax.linalg.triangular_solve(factor, eye, left_side=True, lower=True)  80 us
    all_to_all x1, waiting for transfers between devices, shards(): lax.all_to_all(send_tiles.reshape(owners, CAP, width, width), ('frow', 'f...  76.1 us
    unnamed x32, local copies, waits for them, and re-layouts  64.4 us
    broadcast_in_dim x1, local copies, waits for them, and re-layouts, shards(): return result[None, :, None, :]  20.5 us
    all_gather x1, blocking collectives, shards(): lax.all_gather(first_column[:width].astype(jnp.bfloat16), 'fcol', axis=1,...  18.7 us
    dot_general x1, matrix products, subtract_product(): jnp.dot(row_factor, col_factor.T, precision=lax.Precision.HIGH, preferred...  17.7 us
    dot_general x1, matrix products, shards(): jnp.dot(rows_all, factor_inverse.T, precision=hi, preferred_element_type=...  16.6 us
  transfers between devices with their start and end apart: 7, of which 2 were waited for; matrix products, arithmetic and copies ran while one was open for 59% of the time, Pallas kernels for 0%

commit v1 on v0

--- a/solution.py
+++ b/solution.py
@@ -6,6 +6,14 @@
 PW = 512
 NPANEL = 2
 CAP = 2
+
+
+def gather_from_all(shard, axis, dim):
+    peers = lax.axis_size(axis)
+    repeats = [peers if d == dim else 1 for d in range(shard.ndim)]
+    return lax.all_to_all(
+        jnp.tile(shard, repeats), axis, split_axis=dim, concat_axis=dim, tiled=True
+    )
 
 
 def as_sent(x):
@@ -103,9 +111,7 @@
     global_cols = (local_cols // width * col_devs + col_here) * width + local_cols % width
     total = NPANEL * PW
     hi = lax.Precision.HIGH
-    first_row = lax.all_gather(
-        first_column[:width].astype(jnp.bfloat16), "fcol", axis=1, tiled=True
-    )[:, :total]
+    first_row = gather_from_all(first_column[:width].astype(jnp.bfloat16), "fcol", 1)[:, :total]
     split = total // 2
     left = lax.all_gather(first_row[:, :split], "frow", axis=0, tiled=True)[:total]
     left, right_src, matrix = lax.optimization_barrier((left, first_row[:, split:], matrix))

time: 620 us -> 557 us (0.90)
  local copies, waits for them, and re-layouts: 154 us -> 95.4 us
    unnamed x32 -> x22, local copies, waits for them, and re-layouts: 64.4 us -> 41.5 us
    all_gather x1 -> x0, blocking collectives: 18.7 us -> none  [shards(): lax.all_gather(first_column[:width].astype(jnp.bfloat16), 'fcol', axis=1,...]
    all_to_all x0 -> x1, blocking collectives: none -> 14.8 us  [gather_from_all(): lax.all_to_all(jnp.tile(shard, repeats), axis, split_axis=dim, concat_axi...]
    ppermute x1, waiting for transfers between devices: 16 us -> 3.89 us  [shards(): piece = lax.ppermute(piece, ('frow', 'fcol'), pairs)]
    all_to_all x1, waiting for transfers between devices: 76.1 us -> 85.8 us  [shards(): lax.all_to_all(send_tiles.reshape(owners, CAP, width, width), ('frow', 'f...]
    reshape x1 -> x0, local copies, waits for them, and re-layouts: 9.27 us -> none  [shards(): added = summed.reshape(row_blocks, col_blocks, width, width).transpose(0,...]
    broadcast_in_dim x1, local copies, waits for them, and re-layouts: 20.5 us -> 12.5 us  [shards(): return result[None, :, None, :]]
    another operation x11 -> x9, other arithmetic: 80 us -> 79.3 us  [shards(): lax.linalg.triangular_solve(factor, eye, left_side=True, lower=True)]
  transfers between devices with their start and end apart: 7 -> 7, of which waited for: 2 -> 2; matrix products, arithmetic and copies ran while one was open for 59% -> 60% of each run, Pallas kernels for 0% -> 0%
where the time goes in v1:
time: 557 us; the launch traced here: 549 us
  other arithmetic  223 us (40%)
  local copies, waits for them, and re-layouts  95.4 us (17%)
  waiting for transfers between devices  89.8 us (16%)
  matrix products  85.8 us (15%)
  starting transfers between devices  26.3 us (5%)
  blocking collectives  14.8 us (3%)
  between operations  14.3 us (3%)
    another operation x24, other arithmetic, shards(): factor = jnp.linalg.cholesky(symmetric)  99.9 us
    all_to_all x1, waiting for transfers between devices, shards(): lax.all_to_all(send_tiles.reshape(owners, CAP, width, width), ('frow', 'f...  85.8 us
    another operation x9, other arithmetic, shards(): lax.linalg.triangular_solve(factor, eye, left_side=True, lower=True)  79.3 us
    unnamed x22, local copies, waits for them, and re-layouts  41.5 us
    dot_general x1, matrix products, subtract_product(): jnp.dot(row_factor, col_factor.T, precision=lax.Precision.HIGH, preferred...  18 us
    add x1, other arithmetic, shards(): matrix = local + added  17.4 us
    all_to_all x1, blocking collectives, gather_from_all(): lax.all_to_all(jnp.tile(shard, repeats), axis, split_axis=dim, concat_axi...  14.8 us
    dot_general x1, matrix products, shards(): jnp.dot(rows_all, factor_inverse.T, precision=hi, preferred_element_type=...  14.6 us
  transfers between devices with their start and end apart: 7, of which 2 were waited for; matrix products, arithmetic and copies ran while one was open for 60% of the time, Pallas kernels for 0%

profile of v1, /device:TPU:23, one launch (start us, length us, event | category | flops | bytes accessed | tf_op | source)
XLA Modules:
  0.0 549.3 jit_solution(12780367596143964777)
XLA Ops:
  8.8 1.9 gather_fusion
  11.4 10.6 %all-to-all-start = ((s32[128,1,2]{2,1,0:T(1,128)}), s32[128,1,2]{2,1,0:T(1,128)S(1)}, u32[]{:S(2)}, u32[]{:S(2)}) async-start(s32[128,1,2]{2,1,0:T(1,128)} %bitcast.4), calls=%async_computation | async-start | bytes 131072 | tf_op jit(solution)/shard_map/all_to_all | solution.py:85
  23.1 3.6 fusion.28
  26.8 10.2 %gather_fusion.1 = bf16[256,128,128]{2,1,0:T(8,128)(2,1)} fusion(bf16[64,128,128]{2,1,0:T(8,128)(2,1)} %fusion.28, s32[1024]{0:T(1024)S(1)} %pad_clamp_fusion), kind=kCustom, calls=%fused_computation.1 | custom fusion | bytes 16778240 | tf_op jit(solution)/shard_map/jit(_take)/gather | solution.py:74
  37.0 7.4 %select_select_fusion = bf16[128,2,128,128]{3,2,1,0:T(8,128)(2,1)} fusion(bf16[128,2,128,128]{3,2,1,0:T(8,128)(2,1)} %bitcast.215, pred[128,2]{1,0:T(8,128)(4,1)S(1)} %compare_and_fusion, pred[128,2]{1,0:T(8,128)(4,1)S(1)} %broadcast_in_dim.106), kind=kLoop, calls=%fused_computation.8 | loop fusion | flops 8388608 | bytes 16777728 | tf_op jit(solution)/shard_map/jit(_where)/select_n | solution.py:72
  44.4 10.2 %all-to-all-start.1 = ((bf16[128,2,128,128]{3,2,1,0:T(8,128)(2,1)}), bf16[128,2,128,128]{3,2,1,0:T(8,128)(2,1)}, u32[]{:S(2)}, u32[]{:S(2)}) async-start(bf16[128,2,128,128]{3,2,1,0:T(8,128)(2,1)} %select_select_fusion), calls=%async_computation.1 | async-start | bytes 16777216 | tf_op jit(solution)/shard_map/all_to_all | solution.py:78
  55.2 10.7 %copy.218 = f32[1,1024,1,2048]{3,1,2,0:T(8,128)} copy(f32[1,1024,1,2048]{3,2,1,0:T(1,128)} %param.52) | data formatting | bytes 16777216
  67.3 85.8 %all-to-all-done.1 = bf16[128,2,128,128]{3,2,1,0:T(8,128)(2,1)} async-done(((bf16[128,2,128,128]{3,2,1,0:T(8,128)(2,1)}), bf16[128,2,128,128]{3,2,1,0:T(8,128)(2,1)}, u32[]{:S(2)}, u32[]{:S(2)}) %all-to-all-start.1) | async-done | bytes 8388640 | tf_op jit(solution)/shard_map/all_to_all | solution.py:78
  153.1 7.8 %fusion.139 = f32[8,16384]{1,0:T(8,128)S(1)} fusion(s32[256]{0:T(256)S(1)} %eq.128, s32[8]{0:T(128)S(1)} %iota_multiply_fusion, bf16[32,8,128,128]{3,2,1,0:T(8,128)(2,1)} %bitcast.78), kind=kOutput, calls=%fused_computation.235 | convolution fusion | flops 67110912 | bytes 8913952 | tf_op jit(solution)/shard_map/dot_general | solution.py:104
  162.3 14.8 %all_to_all.20 = bf16[128,8,128]{0,2,1:T(8,128)(2,1)S(1)} all-to-all(bf16[128,8,128]{0,2,1:T(8,128)(2,1)S(1)} %tile.2), channel_id=1, replica_groups=mesh['frow'=16,'fcol'=8] {'fcol'}, dimensions={1} | all-to-all | bytes 524288 | tf_op jit(solution)/shard_map/all_to_all | solution.py:14
  178.3 23.5 %copy.217 = bf16[32,8,128,128]{3,1,2,0:T(8,128)(2,1)} copy(bf16[32,8,128,128]{3,2,1,0:T(8,128)(2,1)} %bitcast.78) | data formatting | bytes 16777216
  201.8 11.9 %copy.142 = bf16[256,16384]{0,1:T(8,128)(2,1)} copy(bf16[256,16384]{1,0:T(8,128)(2,1)} %bitcast.216) | data formatting | bytes 16777216 | tf_op jit(solution)/shard_map/reshape | solution.py:105
  213.8 9.6 %fusion.90 = f32[8,16,128,128]{3,1,2,0:T(8,128)} fusion(bf16[128,128,256,1]{2,1,0,3:T(8,128)(2,1)} %bitcast.219, s32[8,16]{1,0:T(8,128)S(1)} %multiply_add_fusion, s32[256]{0:T(256)S(1)} %eq.128), kind=kOutput, calls=%fused_computation.114 | convolution fusion | flops 1073774592 | bytes 16778752 | tf_op jit(solution)/shard_map/dot_general | solution.py:93
  223.4 17.4 %bitcast_add_fusion = f32[1024,2048]{1,0:T(8,128)} fusion(f32[128,8,16,128]{3,2,1,0:T(8,128)} %bitcast.218, f32[1,1024,1,2048]{3,2,1,0:T(1,128)} %param.52), kind=kLoop, calls=%fused_computation.2 | loop fusion | flops 2097152 | bytes 25165824 | tf_op jit(solution)/shard_map/add | solution.py:101
  240.8 1.3 slice.718
  243.7 11.7 %cholesky.134 = f32[128,128]{1,0:T(8,128)S(1)} custom-call(f32[128,128]{1,0:T(8,128)S(1)} %copy.149), custom_call_target="Cholesky" | custom-call | tf_op jit(solution)/shard_map/jit(cholesky)/cholesky | solution.py:161
  256.8 9.8 %custom-call.12 = f32[1,128,128]{1,2,0:T(8,128)S(1)} custom-call(f32[1,128,128]{2,1,0:T(8,128)S(1)} %get-tuple-element.281), custom_call_target="InvertDiagBlocksLowerTriangular" | custom-call | tf_op jit(solution)/shard_map/triangular_solve/custom-call.0 | solution.py:162
  266.6 2.5 scatter.54
  272.8 12.1 %cholesky.145 = f32[128,128]{1,0:T(8,128)S(1)} custom-call(f32[128,128]{1,0:T(8,128)S(1)} %copy.156), custom_call_target="Cholesky" | custom-call | tf_op jit(solution)/shard_map/jit(cholesky)/cholesky | solution.py:161
  286.8 9.8 %custom-call.13 = f32[1,128,128]{1,2,0:T(8,128)S(1)} custom-call(f32[1,128,128]{2,1,0:T(8,128)S(1)} %get-tuple-element.310), custom_call_target="InvertDiagBlocksLowerTriangular" | custom-call | tf_op jit(solution)/shard_map/triangular_solve/custom-call.0 | solution.py:162
  297.5 1.5 constant_dynamic-update-slice_fusion.5
  300.3 11.7 %cholesky.156 = f32[128,128]{1,0:T(8,128)S(1)} custom-call(f32[128,128]{1,0:T(8,128)S(1)} %copy.163), custom_call_target="Cholesky" | custom-call | tf_op jit(solution)/shard_map/jit(cholesky)/cholesky | solution.py:161
  314.0 9.8 %custom-call.14 = f32[1,128,128]{1,2,0:T(8,128)S(1)} custom-call(f32[1,128,128]{2,1,0:T(8,128)S(1)} %get-tuple-element.308), custom_call_target="InvertDiagBlocksLowerTriangular" | custom-call | tf_op jit(solution)/shard_map/triangular_solve/custom-call.0 | solution.py:162
  324.7 1.4 constant_dynamic-update-slice_fusion.4
  326.9 11.7 %cholesky.167 = f32[128,128]{1,0:T(8,128)S(1)} custom-call(f32[128,128]{1,0:T(8,128)S(1)} %fusion.105), custom_call_target="Cholesky" | custom-call | tf_op jit(solution)/shard_map/jit(cholesky)/cholesky | solution.py:161
  340.6 10.0 %custom-call.15 = f32[1,128,128]{1,2,0:T(8,128)S(1)} custom-call(f32[1,128,128]{2,1,0:T(8,128)S(1)} %get-tuple-element.306), custom_call_target="InvertDiagBlocksLowerTriangular" | custom-call | tf_op jit(solution)/shard_map/triangular_solve/custom-call.0 | solution.py:162
  353.3 5.5 fusion.31
  358.8 1.3 copy-done.2
  361.3 11.7 %cholesky.178 = f32[128,128]{1,0:T(8,128)S(1)} custom-call(f32[128,128]{1,0:T(8,128)S(1)} %fusion.103), custom_call_target="Cholesky" | custom-call | tf_op jit(solution)/shard_map/jit(cholesky)/cholesky | solution.py:161
  374.7 4.7 collective-permute-start
  380.6 9.8 %custom-call.16 = f32[1,128,128]{1,2,0:T(8,128)S(1)} custom-call(f32[1,128,128]{2,1,0:T(8,128)S(1)} %get-tuple-element.304), custom_call_target="InvertDiagBlocksLowerTriangular" | custom-call | tf_op jit(solution)/shard_map/triangular_solve/custom-call.0 | solution.py:162
  390.7 3.9 collective-permute-done
  395.3 1.9 constant_dynamic-update-slice_fusion.3
  397.3 1.7 fusion.37
  399.3 11.7 %cholesky.189 = f32[128,128]{1,0:T(8,128)S(1)} custom-call(f32[128,128]{1,0:T(8,128)S(1)} %fusion.101), custom_call_target="Cholesky" | custom-call | tf_op jit(solution)/shard_map/jit(cholesky)/cholesky | solution.py:161
  412.9 9.8 %custom-call.17 = f32[1,128,128]{1,2,0:T(8,128)S(1)} custom-call(f32[1,128,128]{2,1,0:T(8,128)S(1)} %get-tuple-element.302), custom_call_target="InvertDiagBlocksLowerTriangular" | custom-call | tf_op jit(solution)/shard_map/triangular_solve/custom-call.0 | solution.py:162
  424.7 12.1 %cholesky.200 = f32[128,128]{1,0:T(8,128)S(1)} custom-call(f32[128,128]{1,0:T(8,128)S(1)} %fusion.99), custom_call_target="Cholesky" | custom-call | tf_op jit(solution)/shard_map/jit(cholesky)/cholesky | solution.py:161
  438.6 9.8 %custom-call.18 = f32[1,128,128]{1,2,0:T(8,128)S(1)} custom-call(f32[1,128,128]{2,1,0:T(8,128)S(1)} %get-tuple-element.300), custom_call_target="InvertDiagBlocksLowerTriangular" | custom-call | tf_op jit(solution)/shard_map/triangular_solve/custom-call.0 | solution.py:162
  450.2 11.7 %cholesky.211 = f32[128,128]{1,0:T(8,128)S(1)} custom-call(f32[128,128]{1,0:T(8,128)S(1)} %fusion.97), custom_call_target="Cholesky" | custom-call | tf_op jit(solution)/shard_map/jit(cholesky)/cholesky | solution.py:161
  463.8 9.8 %custom-call.19 = f32[1,128,128]{1,2,0:T(8,128)S(1)} custom-call(f32[1,128,128]{2,1,0:T(8,128)S(1)} %get-tuple-element.298), custom_call_target="InvertDiagBlocksLowerTriangular" | custom-call | tf_op jit(solution)/shard_map/triangular_solve/custom-call.0 | solution.py:162
  479.6 3.1 fusion.42
  482.7 1.8 fusion.35
  484.6 1.5 fusion.163
  486.1 2.8 copy.143
  489.6 14.6 %fusion.2 = f32[3072,1024]{1,0:T(8,128)S(1)} fusion(bf16[2048,1024]{1,0:T(8,128)(2,1)S(1)} %bitcast.221, bf16[1024,1024]{1,0:T(8,128)(2,1)S(1)} %copy-done.9, f32[1,512,512]{2,1,0:T(8,128)S(1)} %copy-done.7, f32[1,512,512]{2,1,0:T(8,128)S(1)} %copy-done.6, f32[1,512,512]{2,1,0:T(8,128)S(1)} %fusion.35), kind=kOutput, calls=%fused_computation.9 | convolution fusion | flops 19344130048 | bytes 22020096 | tf_op jit(solution)/shard_map/dot_general | solution.py:208
  504.2 4.6 copy-done.4
  509.2 18.0 %fusion.15 = f32[1024,2048]{1,0:T(8,128)S(1)} fusion(f32[1024,2048]{1,0:T(8,128)} %bitcast_add_fusion, f32[3072,1024]{1,0:T(8,128)} %copy-done.4), kind=kOutput, calls=%fused_computation.27 | convolution fusion | flops 12886999040 | bytes 29360128 | tf_op jit(solution)/shard_map/dot_general | solution.py:44
  530.0 12.5 %copy.186 = f32[1,1024,1,2048]{3,2,1,0:T(1,128)} copy(f32[1,1024,1,2048]{3,1,2,0:T(8,128)S(1)} %select_bitcast_fusion) | data formatting | bytes 16777216 | tf_op jit(solution)/shard_map/broadcast_in_dim | solution.py:221
  (168 shorter events, 51.7 us)
Async XLA Ops:
  6.5 16.6 %copy-start = (bf16[64,128,128]{2,1,0:T(8,128)(2,1)S(1)}, bf16[64,128,128]{2,1,0:T(8,128)(2,1)}, u32[]{:S(2)}) copy-start(bf16[64,128,128]{2,1,0:T(8,128)(2,1)} %param.53) | copy-start | bytes 6291460
  11.4 33.0 %all-to-all-start = ((s32[128,1,2]{2,1,0:T(1,128)}), s32[128,1,2]{2,1,0:T(1,128)S(1)}, u32[]{:S(2)}, u32[]{:S(2)}) async-start(s32[128,1,2]{2,1,0:T(1,128)} %bitcast.4), calls=%async_computation | async-start | bytes 131072 | tf_op jit(solution)/shard_map/all_to_all | solution.py:85
  44.4 108.7 %all-to-all-start.1 = ((bf16[128,2,128,128]{3,2,1,0:T(8,128)(2,1)}), bf16[128,2,128,128]{3,2,1,0:T(8,128)(2,1)}, u32[]{:S(2)}, u32[]{:S(2)}) async-start(bf16[128,2,128,128]{3,2,1,0:T(8,128)(2,1)} %select_select_fusion), calls=%async_computation.1 | async-start | bytes 16777216 | tf_op jit(solution)/shard_map/all_to_all | solution.py:78
  54.6 186.1 %all-gather.6.cloned.1.call-start = ((), (), s32[]{:S(2)}) async-start(), calls=%async_computation.3 | async-start | bytes 2228224 | tf_op jit(solution)/shard_map/all_gather | solution.py:116
  162.1 39.7 %copy-start.5 = (bf16[1024,128]{1,0:T(8,128)(2,1)}, bf16[1024,128]{1,0:T(8,128)(2,1)S(1)}, u32[]{:S(2)}) copy-start(bf16[1024,128]{1,0:T(8,128)(2,1)S(1)} %slice_add_fusion) | copy-start | bytes 786436
  177.8 122.3 %all-gather.8.cloned.1.call-start = ((), (), s32[]{:S(2)}) async-start(), calls=%async_computation.4 | async-start | bytes 2228224 | tf_op jit(solution)/shard_map/all_gather | solution.py:118
  242.1 131.6 %all-gather.10.cloned.1.call-start = ((), (), s32[]{:S(2)}) async-start(), calls=%async_computation.5 | async-start | bytes 2359296 | tf_op jit(solution)/shard_map/all_gather | solution.py:121
  300.1 52.6 %slice-start = ((bf16[2048,512]{0,1:T(8,128)(2,1)}), bf16[1024,512]{0,1:T(8,128)(2,1)S(1)}, s32[]{:S(2)}) async-start(bf16[2048,512]{0,1:T(8,128)(2,1)} %all-gather.8.cloned.1.call-done), calls=%async_computation.7 | async-start | bytes 2097152 | tf_op jit(solution)/shard_map/slice | solution.py:118
  300.2 185.9 %all-gather.12.cloned.1.call-start = ((), (), s32[]{:S(2)}) async-start(), calls=%async_computation.6 | async-start | bytes 4456448 | tf_op jit(solution)/shard_map/all_gather | solution.py:133
  353.3 37.1 %copy-start.3 = (f32[8,128,128]{2,1,0:T(8,128)S(1)}, f32[8,128,128]{2,1,0:T(8,128)}, u32[]{:S(2)}) copy-start(f32[8,128,128]{2,1,0:T(8,128)} %get-tuple-element.327) | copy-start | bytes 1572868
  358.8 1.3 copy-start.2
  374.7 19.9 %collective-permute-start = (bf16[128,1024]{1,0:T(8,128)(2,1)S(1)}, bf16[128,1024]{1,0:T(8,128)(2,1)S(1)}, u32[]{:S(2)}, u32[]{:S(2)}) collective-permute-start(bf16[128,1024]{1,0:T(8,128)(2,1)S(1)} %constant_dynamic-slice_fusion), channel_id=1, source_target_pairs={{0,0},{1,8},{2,16},{3,24},{4,32},{5,40},{6,48},{7,56},{8,1},{9,9},... | collective-permute-start | bytes 786440 | tf_op jit(solution)/shard_map/ppermute | solution.py:132
  394.6 0.7 copy-start.8
  486.1 2.8 copy-start.6
  486.1 2.9 copy-start.7
  486.1 3.5 copy-start.9
  504.2 4.6 copy-start.4
  530.0 12.5 %copy-start.1 = (bf16[64,128,128]{2,1,0:T(8,128)(2,1)S(1)}, bf16[64,128,128]{2,1,0:T(8,128)(2,1)}, u32[]{:S(2)}) copy-start(bf16[64,128,128]{2,1,0:T(8,128)(2,1)} %param.53) | copy-start | bytes 6291460
Sparse Core Ops, SparseCore 0:
  177.9 46.6 all-gather.5
  242.2 47.1 all-gather.7
  300.3 28.9 all-gather.9
  395.5 51.5 all-gather.11
